TPU v7x, 32 devices: a whole 2x2x4 slice. The times are simulated.
32 devices in a mesh: groups: 2 (over y), tm: 4 (over x, core), width: 4 (over z).
Axes of the slice: x: 2, y: 2, z: 4, core: 2. Of those that a mesh axis runs over, the one named last changes fastest.
Arguments:
- video: bfloat16 [32, 12, 48, 256], P(('groups', 'tm'), None, 'width'), parts along dimension 0, may hold values from -6 to 6
- conv_w: bfloat16 [2, 3, 3, 256, 256], replicated, may hold values from -0.125 to 0.125
- depth_k: float32 [2, 16, 256], replicated, may hold values from -1.5 to 1.5
- proj_w: bfloat16 [2, 256, 256], replicated, may hold values from -0.375 to 0.375
Outputs:
- result: bfloat16 [32, 12, 48, 256], P(('groups', 'tm'), None, 'width'), parts along dimension 0
There are 2 independent parts, one for each index of `groups`. A program takes and returns all parts, laid end to end along the dimension named above; an argument that names none is the same for every part. Nothing has to cross between parts.
All inputs are finite; a program needn't handle non-finite values.
Results may differ from a plain program's by a relative error of at most 0.0058.
Values may be sent and summed in bfloat16 or wider, within the bound.
No kernel may reach another device: no remote copies, remote signals or barrier semaphores. Data moves between devices by JAX's collectives and lax.ppermute only.
A program may use at most 64 MiB of HBM per device.

v0:
```python
import jax
import jax.numpy as jnp
from jax import lax
from jax.sharding import PartitionSpec as P

BLOCKS = 2


def conv3x3(x, weight):
    return lax.conv_general_dilated(
        x,
        weight,
        window_strides=(1, 1),
        padding="VALID",
        dimension_numbers=("NHWC", "HWIO", "NHWC"),
        preferred_element_type=jnp.float32,
    )


def block(x, weight, kernel, proj):
    chans = x.shape[-1]
    hidden = jax.nn.silu(conv3x3(x, weight)).astype(jnp.bfloat16)
    frames = hidden.shape[0]
    values = hidden.astype(jnp.float32)
    depth = values * kernel[0]
    for lag in range(1, frames):
        shifted = jnp.pad(values[: frames - lag], ((lag, 0), (0, 0), (0, 0), (0, 0)))
        depth = depth + shifted * kernel[lag]
    depth = depth.astype(jnp.bfloat16)
    mixed = jnp.dot(depth.reshape(-1, chans), proj, preferred_element_type=jnp.float32)
    mixed = mixed.reshape(hidden.shape).astype(jnp.bfloat16)
    inner = x[:, 1:-1, 1:-1, :]
    return (inner.astype(jnp.float32) + mixed.astype(jnp.float32)).astype(jnp.bfloat16)


def shards(video, conv_w, depth_k, proj_w):
    bands = lax.axis_size("tm")
    sides = lax.axis_size("width")
    band = lax.axis_index("tm")
    side = lax.axis_index("width")
    frames, height, cols, chans = video.shape
    rows = height // bands
    halo = BLOCKS
    padded = jnp.pad(video, ((0, 0), (halo, halo), (0, 0), (0, 0)))
    pieces = jnp.stack([padded[:, r * rows : r * rows + rows + 2 * halo] for r in range(bands)])
    gathered = lax.all_to_all(pieces, "tm", 0, 0, tiled=False)
    gathered = gathered.reshape(bands * frames, rows + 2 * halo, cols, chans)
    up = [(i, i + 1) for i in range(sides - 1)]
    down = [(i + 1, i) for i in range(sides - 1)]
    before = lax.ppermute(gathered[:, :, cols - halo :], "width", up)
    after = lax.ppermute(gathered[:, :, :halo], "width", down)
    inner = block(gathered, conv_w[0], depth_k[0], proj_w[0])
    reach = 2 * halo
    rims = jnp.concatenate(
        [before, gathered[:, :, :reach], gathered[:, :, cols - reach :], after], axis=2
    )
    rims = block(rims, conv_w[0], depth_k[0], proj_w[0])
    state = jnp.concatenate([rims[:, :, :halo], inner, rims[:, :, rims.shape[2] - halo :]], axis=2)
    for b in range(1, BLOCKS):
        left = halo - b
        n_rows, n_cols = (state.shape[1], state.shape[2])
        row = band * rows - left + lax.broadcasted_iota(jnp.int32, (n_rows, n_cols), 0)
        col = side * cols - left + lax.broadcasted_iota(jnp.int32, (n_rows, n_cols), 1)
        inside = (row >= 0) & (row < height) & (col >= 0) & (col < sides * cols)
        state = jnp.where(inside[None, :, :, None], state, jnp.zeros((), state.dtype))
        state = block(state, conv_w[b], depth_k[b], proj_w[b])
    return lax.all_to_all(state, "tm", 0, 1, tiled=True)


def solution(mesh):
    return jax.shard_map(
        shards,
        mesh=mesh,
        in_specs=(P(("groups", "tm"), None, "width", None), P(), P(), P()),
        out_specs=P(("groups", "tm"), None, "width", None),
        check_vma=False,
    )
```

profile of v0, /device:TPU:0, one launch (start us, length us, event | category | flops | bytes accessed | tf_op | source)
XLA Modules:
  0.0 48.9 jit_solution(6434809782838823936)
XLA Ops:
  0.0 0.0 copy-start
  0.0 1.4 %fusion.38 = (bf16[1,4,7,12,256]{4,1,3,2,0:T(4,128)(2,1)S(1)}, bf16[1,4,7,12,256]{4,1,3,2,0:T(4,128)(2,1)S(1)}, bf16[1,4,7,12,256]{4,1,3,2,0:T(4,128)(2,1)S(1)}, bf16[1,4,7,12,256]{4,1,3,2,0:T(4,128)(2,1)S(1)}) fusion(bf16[4,12,12,256]{3,0,2,1:T(4,128)(2,1)} %param.4), kind=kLoop, calls=%fused_computation.40 | loop fusion | bytes 1327104 | tf_op jit(solution)/shard_map/stack | solution.py:45
  1.4 1.5 %pad_maximum_fusion = bf16[4,4,7,12,256]{4,1,3,2,0:T(4,128)(2,1)} fusion(bf16[1,4,7,12,256]{4,1,3,2,0:T(4,128)(2,1)S(1)} %get-tuple-element.12, bf16[1,4,7,12,256]{4,1,3,2,0:T(4,128)(2,1)S(1)} %get-tuple-element.13, bf16[1,4,7,12,256]{4,1,3,2,0:T(4,128)(2,1)S(1)} %get-tuple-element.14, bf16[1,4,7,12,256]{4,1,3,2,0:T(4,128)(2,1)S(1)} %get-tuple-element.11), kind=kLoop, calls=%fused_computation.26 | loop fusion | flops 1032192 | bytes 1376256 | tf_op jit(solution)/shard_map/stack | solution.py:45
  2.8 4.2 %all-to-all-start = ((bf16[4,4,7,12,256]{4,1,3,2,0:T(4,128)(2,1)}), bf16[4,4,7,12,256]{4,1,3,2,0:T(4,128)(2,1)S(1)}, u32[]{:S(2)}, u32[]{:S(2)}) async-start(bf16[4,4,7,12,256]{4,1,3,2,0:T(4,128)(2,1)} %pad_maximum_fusion), calls=%async_computation | async-start | bytes 1376256 | tf_op jit(solution)/shard_map/all_to_all | solution.py:46
  7.1 0.1 and_and_fusion
  7.2 0.0 copy-done
  7.2 10.4 %all-to-all-done = bf16[4,4,7,12,256]{4,1,3,2,0:T(4,128)(2,1)S(1)} async-done(((bf16[4,4,7,12,256]{4,1,3,2,0:T(4,128)(2,1)}), bf16[4,4,7,12,256]{4,1,3,2,0:T(4,128)(2,1)S(1)}, u32[]{:S(2)}, u32[]{:S(2)}) %all-to-all-start) | async-done | bytes 688160 | tf_op jit(solution)/shard_map/all_to_all | solution.py:46
  17.7 0.3 copy.7
  17.9 0.2 reshape.154
  18.1 2.4 %fusion.18 = f32[16,5,10,256]{3,0,2,1:T(8,128)S(1)} fusion(bf16[16,7,12,256]{3,0,2,1:T(8,128)(2,1)S(1)} %reshape.154, bf16[2,3,3,256,256]{4,3,2,1,0:T(8,128)(2,1)} %param.5), kind=kOutput, calls=%fused_computation.21 | convolution fusion | flops 944947200 | bytes 2686976 | tf_op jit(solution)/shard_map/conv_general_dilated | solution.py:10
  20.5 0.0 copy-start.2
  20.8 4.2 %collective-permute-start = (bf16[16,7,2,256]{3,0,2,1:T(8,128)(2,1)S(1)}, bf16[16,7,2,256]{3,0,2,1:T(8,128)(2,1)S(1)}, u32[]{:S(2)}, u32[]{:S(2)}) collective-permute-start(bf16[16,7,2,256]{3,0,2,1:T(8,128)(2,1)S(1)} %get-tuple-element.5), channel_id=1, source_target_pairs={{0,1},{1,2},{2,3},{4,5},{5,6},{6,7},{8,9},{9,10},{10,11},{12,13},{... | collective-permute-start | bytes 344072 | tf_op jit(solution)/shard_map/ppermute | solution.py:50
  25.0 1.3 %collective-permute-start.1 = (bf16[16,7,2,256]{3,0,2,1:T(8,128)(2,1)S(1)}, bf16[16,7,2,256]{3,0,2,1:T(8,128)(2,1)S(1)}, u32[]{:S(2)}, u32[]{:S(2)}) collective-permute-start(bf16[16,7,2,256]{3,0,2,1:T(8,128)(2,1)S(1)} %get-tuple-element.6), channel_id=1, source_target_pairs={{1,0},{2,1},{3,2},{5,4},{6,5},{7,6},{9,8},{10,9},{11,10},{13,12},{... | collective-permute-start | bytes 344072 | tf_op jit(solution)/shard_map/ppermute | solution.py:51
  26.3 0.0 copy-done.2
  26.3 0.0 copy-start.1
  26.3 2.0 %fusion.2 = bf16[16,5,10,256]{3,0,2,1:T(8,128)(2,1)S(1)} fusion(bf16[16,7,12,256]{3,0,2,1:T(8,128)(2,1)S(1)} %reshape.154, f32[1,5,10,256]{3,0,2,1:T(1,128)S(1)} %slice.498, f32[2,5,10,256]{3,0,2,1:T(2,128)S(1)} %slice.497, f32[3,5,10,256]{3,0,2,1:T(4,128)S(1)} %slice.496, f32[4,5,10,256]{3,0,2,1:T(4,128)S(1)} %slice.495, f32[5,5,10,256]{3,0,2,1:T(8,128)S(1)} %slice.494, ...), kind=kOutput, calls=%fused_computation.3 | convolution fusion | flops 112435200 | bytes 9721856 | tf_op jit(solution)/shard_map/dot_general | solution.py:30
  28.3 0.0 collective-permute-done
  28.3 3.4 %collective-permute-done.1 = bf16[16,7,2,256]{3,0,2,1:T(8,128)(2,1)S(1)} collective-permute-done((bf16[16,7,2,256]{3,0,2,1:T(8,128)(2,1)S(1)}, bf16[16,7,2,256]{3,0,2,1:T(8,128)(2,1)S(1)}, u32[]{:S(2)}, u32[]{:S(2)}) %collective-permute-start.1) | collective-permute-done | bytes 114720 | tf_op jit(solution)/shard_map/ppermute | solution.py:51
  31.7 0.0 copy-done.1
  31.7 1.1 %fusion.23 = f32[16,5,10,256]{3,0,2,1:T(8,128)S(1)} fusion(bf16[2,3,3,256,256]{4,3,2,1,0:T(8,128)(2,1)S(1)} %copy-done.1, bf16[16,7,2,256]{3,0,2,1:T(8,128)(2,1)S(1)} %collective-permute-done.1, bf16[16,7,4,256]{3,0,2,1:T(8,128)(2,1)S(1)} %get-tuple-element.8, bf16[16,7,4,256]{3,0,2,1:T(8,128)(2,1)S(1)} %get-tuple-element.7, ...), kind=kOutput, calls=%fused_computation.25 | convolution fusion | flops 945979392 | bytes 2686976 | tf_op jit(solution)/shard_map/conv_general_dilated | solution.py:10
  33.1 2.3 %add_convert_fusion.1 = bf16[16,5,10,256]{3,0,2,1:T(8,128)(2,1)S(1)} fusion(bf16[16,7,2,256]{3,0,2,1:T(8,128)(2,1)S(1)} %collective-permute-done.1, bf16[16,7,4,256]{3,0,2,1:T(8,128)(2,1)S(1)} %get-tuple-element.8, bf16[16,7,4,256]{3,0,2,1:T(8,128)(2,1)S(1)} %get-tuple-element.7, bf16[16,7,2,256]{3,0,2,1:T(8,128)(2,1)S(1)} %collective-permute-done, ...), kind=kOutput, calls=%fused_computation.22 | convolution fusion | flops 113049600 | bytes 10000384 | tf_op jit(solution)/shard_map/dot_general | solution.py:30
  35.5 0.1 maximum_select_fusion
  35.6 0.9 %fusion.35 = f32[16,3,12,256]{3,0,2,1:T(8,128)S(1)} fusion(bf16[16,5,14,256]{3,0,2,1:T(8,128)(2,1)S(1)} %maximum_select_fusion, bf16[2,3,3,256,256]{4,3,2,1,0:T(8,128)(2,1)S(1)} %copy-done.1), kind=kOutput, calls=%fused_computation.36 | convolution fusion | flops 680361984 | bytes 2342912 | tf_op jit(solution)/shard_map/conv_general_dilated | solution.py:10
  36.7 1.4 %fusion.6 = bf16[16,3,12,256]{3,0,2,1:T(8,128)(2,1)S(1)} fusion(bf16[16,5,14,256]{3,0,2,1:T(8,128)(2,1)S(1)} %maximum_select_fusion, f32[1,3,12,256]{3,0,2,1:T(1,128)S(1)} %slice.515, f32[2,3,12,256]{3,0,2,1:T(2,128)S(1)} %slice.514, f32[3,3,12,256]{3,0,2,1:T(4,128)S(1)} %slice.513, f32[4,3,12,256]{3,0,2,1:T(4,128)S(1)} %slice.512, ...), kind=kOutput, calls=%fused_computation.9 | convolution fusion | flops 80953344 | bytes 7041024 | tf_op jit(solution)/shard_map/dot_general | solution.py:30
  38.2 0.1 copy.8
  38.3 9.8 %all_to_all.23 = bf16[16,3,12,256]{3,2,1,0:T(8,128)(2,1)S(1)} all-to-all(bf16[16,3,12,256]{3,2,1,0:T(8,128)(2,1)S(1)} %copy.8), channel_id=1, replica_groups=mesh['groups'=2,'tm'=4,'width'=4] {'tm'}, dimensions={0} | all-to-all | bytes 589824 | tf_op jit(solution)/shard_map/all_to_all | solution.py:67
  48.1 0.9 %copy.9 = bf16[4,4,3,12,256]{4,0,3,2,1:T(4,128)(2,1)} copy(bf16[4,4,3,12,256]{4,3,2,0,1:T(8,128)(2,1)S(1)} %bitcast.126) | data formatting | bytes 589824 | tf_op jit(solution)/shard_map/all_to_all | solution.py:67
  (31 shorter events, 0.7 us)
Async XLA Ops:
  0.0 7.2 %copy-start = (f32[2,16,256]{2,1,0:T(8,128)S(1)}, f32[2,16,256]{2,1,0:T(8,128)}, u32[]{:S(2)}) copy-start(f32[2,16,256]{2,1,0:T(8,128)} %param.6) | copy-start | bytes 98308
  2.8 14.8 %all-to-all-start = ((bf16[4,4,7,12,256]{4,1,3,2,0:T(4,128)(2,1)}), bf16[4,4,7,12,256]{4,1,3,2,0:T(4,128)(2,1)S(1)}, u32[]{:S(2)}, u32[]{:S(2)}) async-start(bf16[4,4,7,12,256]{4,1,3,2,0:T(4,128)(2,1)} %pad_maximum_fusion), calls=%async_computation | async-start | bytes 1376256 | tf_op jit(solution)/shard_map/all_to_all | solution.py:46
  20.5 5.8 %copy-start.2 = (bf16[2,256,256]{2,1,0:T(8,128)(2,1)S(1)}, bf16[2,256,256]{2,1,0:T(8,128)(2,1)}, u32[]{:S(2)}) copy-start(bf16[2,256,256]{2,1,0:T(8,128)(2,1)} %param.7) | copy-start | bytes 786436
  20.8 7.5 %collective-permute-start = (bf16[16,7,2,256]{3,0,2,1:T(8,128)(2,1)S(1)}, bf16[16,7,2,256]{3,0,2,1:T(8,128)(2,1)S(1)}, u32[]{:S(2)}, u32[]{:S(2)}) collective-permute-start(bf16[16,7,2,256]{3,0,2,1:T(8,128)(2,1)S(1)} %get-tuple-element.5), channel_id=1, source_target_pairs={{0,1},{1,2},{2,3},{4,5},{5,6},{6,7},{8,9},{9,10},{10,11},{12,13},{... | collective-permute-start | bytes 344072 | tf_op jit(solution)/shard_map/ppermute | solution.py:50
  25.0 6.7 %collective-permute-start.1 = (bf16[16,7,2,256]{3,0,2,1:T(8,128)(2,1)S(1)}, bf16[16,7,2,256]{3,0,2,1:T(8,128)(2,1)S(1)}, u32[]{:S(2)}, u32[]{:S(2)}) collective-permute-start(bf16[16,7,2,256]{3,0,2,1:T(8,128)(2,1)S(1)} %get-tuple-element.6), channel_id=1, source_target_pairs={{1,0},{2,1},{3,2},{5,4},{6,5},{7,6},{9,8},{10,9},{11,10},{13,12},{... | collective-permute-start | bytes 344072 | tf_op jit(solution)/shard_map/ppermute | solution.py:51
  26.3 5.4 %copy-start.1 = (bf16[2,3,3,256,256]{4,3,2,1,0:T(8,128)(2,1)S(1)}, bf16[2,3,3,256,256]{4,3,2,1,0:T(8,128)(2,1)}, u32[]{:S(2)}) copy-start(bf16[2,3,3,256,256]{4,3,2,1,0:T(8,128)(2,1)} %param.5) | copy-start | bytes 7077892
where the time goes:
time: 49.2 us; the launch traced here: 48.9 us
  waiting for transfers between devices  13.8 us (28%)
  matrix products  10.1 us (21%)
  blocking collectives  9.8 us (20%)
  starting transfers between devices  9.71 us (20%)
  local copies, waits for them, and re-layouts  3.47 us (7%)
  other arithmetic  1.71 us (3%)
    all_to_all x1, waiting for transfers between devices, shards(): gathered = lax.all_to_all(pieces, 'tm', 0, 0, tiled=False)  10.4 us
    all_to_all x1, blocking collectives, shards(): return lax.all_to_all(state, 'tm', 0, 1, tiled=True)  9.8 us
    dot_general x3, matrix products, block(): jnp.dot(depth.reshape(-1, chans), proj, preferred_element_type=jnp.float32)  5.69 us
    conv_general_dilated x3, matrix products, conv3x3(): lax.conv_general_dilated(x, weight, window_strides=(1, 1), padding='VALID...  4.41 us
    all_to_all x1, starting transfers between devices, shards(): gathered = lax.all_to_all(pieces, 'tm', 0, 0, tiled=False)  4.24 us
    ppermute x1, starting transfers between devices, shards(): before = lax.ppermute(gathered[:, :, cols - halo:], 'width', up)  4.18 us
    ppermute x1, waiting for transfers between devices, shards(): after = lax.ppermute(gathered[:, :, :halo], 'width', down)  3.36 us
    another operation x1, other arithmetic, shards(): jnp.stack([padded[:, r * rows:r * rows + rows + 2 * halo] for r in range(...  1.47 us
  transfers between devices with their start and end apart: 3, of which 2 were waited for; matrix products, arithmetic and copies ran while one was open for 4% of the time, Pallas kernels for 0%

commit v1 on v0

--- a/solution.py
+++ b/solution.py
@@ -64,7 +64,9 @@
         inside = (row >= 0) & (row < height) & (col >= 0) & (col < sides * cols)
         state = jnp.where(inside[None, :, :, None], state, jnp.zeros((), state.dtype))
         state = block(state, conv_w[b], depth_k[b], proj_w[b])
-    return lax.all_to_all(state, "tm", 0, 1, tiled=True)
+    return jnp.concatenate(
+        lax.all_to_all(jnp.stack(jnp.split(state, lax.axis_size("tm"), axis=0)), "tm", 0, 0), axis=1
+    )
 
 
 def solution(mesh):

time: 49.2 us -> 48.3 us (0.982)
  blocking collectives: 9.8 us -> 8.72 us
    all_to_all x1, blocking collectives: 9.8 us -> 8.72 us  [shards(): lax.all_to_all(jnp.stack(jnp.split(state, lax.axis_size('tm'), axis=0)),...]
    all_to_all x1 -> x0, local copies, waits for them, and re-layouts: 0.87 us -> none  [shards(): return lax.all_to_all(state, 'tm', 0, 1, tiled=True)]
    unnamed x6 -> x7, local copies, waits for them, and re-layouts: 0.02 us -> 0.73 us
where the time goes in v1:
time: 48.3 us; the launch traced here: 48 us
  waiting for transfers between devices  13.8 us (29%)
  matrix products  10.1 us (21%)
  starting transfers between devices  9.72 us (20%)
  blocking collectives  8.72 us (18%)
  local copies, waits for them, and re-layouts  3.32 us (7%)
  other arithmetic  1.99 us (4%)
    all_to_all x1, waiting for transfers between devices, shards(): gathered = lax.all_to_all(pieces, 'tm', 0, 0, tiled=False)  10.4 us
    all_to_all x1, blocking collectives, shards(): lax.all_to_all(jnp.stack(jnp.split(state, lax.axis_size('tm'), axis=0)),...  8.72 us
    dot_general x3, matrix products, block(): jnp.dot(depth.reshape(-1, chans), proj, preferred_element_type=jnp.float32)  5.69 us
    conv_general_dilated x3, matrix products, conv3x3(): lax.conv_general_dilated(x, weight, window_strides=(1, 1), padding='VALID...  4.41 us
    all_to_all x1, starting transfers between devices, shards(): gathered = lax.all_to_all(pieces, 'tm', 0, 0, tiled=False)  4.24 us
    ppermute x1, starting transfers between devices, shards(): before = lax.ppermute(gathered[:, :, cols - halo:], 'width', up)  4.19 us
    ppermute x1, waiting for transfers between devices, shards(): after = lax.ppermute(gathered[:, :, :halo], 'width', down)  3.36 us
    another operation x1, other arithmetic, shards(): jnp.stack([padded[:, r * rows:r * rows + rows + 2 * halo] for r in range(...  1.48 us
  transfers between devices with their start and end apart: 3, of which 2 were waited for; matrix products, arithmetic and copies ran while one was open for 4% of the time, Pallas kernels for 0%

profile of v1, /device:TPU:0, one launch (start us, length us, event | category | flops | bytes accessed | tf_op | source)
XLA Modules:
  0.0 48.0 jit_solution(4058733956180179016)
XLA Ops:
  0.0 0.0 copy-start
  0.0 1.4 %fusion.38 = (bf16[1,4,7,12,256]{4,1,3,2,0:T(4,128)(2,1)S(1)}, bf16[1,4,7,12,256]{4,1,3,2,0:T(4,128)(2,1)S(1)}, bf16[1,4,7,12,256]{4,1,3,2,0:T(4,128)(2,1)S(1)}, bf16[1,4,7,12,256]{4,1,3,2,0:T(4,128)(2,1)S(1)}) fusion(bf16[4,12,12,256]{3,0,2,1:T(4,128)(2,1)} %param.4), kind=kLoop, calls=%fused_computation.41 | loop fusion | bytes 1327104 | tf_op jit(solution)/shard_map/stack | solution.py:45
  1.4 1.5 %pad_maximum_fusion = bf16[4,4,7,12,256]{4,1,3,2,0:T(4,128)(2,1)} fusion(bf16[1,4,7,12,256]{4,1,3,2,0:T(4,128)(2,1)S(1)} %get-tuple-element.16, bf16[1,4,7,12,256]{4,1,3,2,0:T(4,128)(2,1)S(1)} %get-tuple-element.17, bf16[1,4,7,12,256]{4,1,3,2,0:T(4,128)(2,1)S(1)} %get-tuple-element.18, bf16[1,4,7,12,256]{4,1,3,2,0:T(4,128)(2,1)S(1)} %get-tuple-element.15), kind=kLoop, calls=%fused_computation.26 | loop fusion | flops 1032192 | bytes 1376256 | tf_op jit(solution)/shard_map/stack | solution.py:45
  2.9 4.2 %all-to-all-start = ((bf16[4,4,7,12,256]{4,1,3,2,0:T(4,128)(2,1)}), bf16[4,4,7,12,256]{4,1,3,2,0:T(4,128)(2,1)S(1)}, u32[]{:S(2)}, u32[]{:S(2)}) async-start(bf16[4,4,7,12,256]{4,1,3,2,0:T(4,128)(2,1)} %pad_maximum_fusion), calls=%async_computation | async-start | bytes 1376256 | tf_op jit(solution)/shard_map/all_to_all | solution.py:46
  7.1 0.1 and_and_fusion
  7.2 0.0 copy-done
  7.2 10.4 %all-to-all-done = bf16[4,4,7,12,256]{4,1,3,2,0:T(4,128)(2,1)S(1)} async-done(((bf16[4,4,7,12,256]{4,1,3,2,0:T(4,128)(2,1)}), bf16[4,4,7,12,256]{4,1,3,2,0:T(4,128)(2,1)S(1)}, u32[]{:S(2)}, u32[]{:S(2)}) %all-to-all-start) | async-done | bytes 688160 | tf_op jit(solution)/shard_map/all_to_all | solution.py:46
  17.7 0.3 copy.5
  17.9 0.2 reshape.160
  18.1 2.4 %fusion.18 = f32[16,5,10,256]{3,0,2,1:T(8,128)S(1)} fusion(bf16[16,7,12,256]{3,0,2,1:T(8,128)(2,1)S(1)} %reshape.160, bf16[2,3,3,256,256]{4,3,2,1,0:T(8,128)(2,1)} %param.5), kind=kOutput, calls=%fused_computation.21 | convolution fusion | flops 944947200 | bytes 2686976 | tf_op jit(solution)/shard_map/conv_general_dilated | solution.py:10
  20.5 0.0 copy-start.2
  20.8 4.2 %collective-permute-start = (bf16[16,7,2,256]{3,0,2,1:T(8,128)(2,1)S(1)}, bf16[16,7,2,256]{3,0,2,1:T(8,128)(2,1)S(1)}, u32[]{:S(2)}, u32[]{:S(2)}) collective-permute-start(bf16[16,7,2,256]{3,0,2,1:T(8,128)(2,1)S(1)} %get-tuple-element.5), channel_id=1, source_target_pairs={{0,1},{1,2},{2,3},{4,5},{5,6},{6,7},{8,9},{9,10},{10,11},{12,13},{... | collective-permute-start | bytes 344072 | tf_op jit(solution)/shard_map/ppermute | solution.py:50
  25.0 1.3 %collective-permute-start.1 = (bf16[16,7,2,256]{3,0,2,1:T(8,128)(2,1)S(1)}, bf16[16,7,2,256]{3,0,2,1:T(8,128)(2,1)S(1)}, u32[]{:S(2)}, u32[]{:S(2)}) collective-permute-start(bf16[16,7,2,256]{3,0,2,1:T(8,128)(2,1)S(1)} %get-tuple-element.6), channel_id=1, source_target_pairs={{1,0},{2,1},{3,2},{5,4},{6,5},{7,6},{9,8},{10,9},{11,10},{13,12},{... | collective-permute-start | bytes 344072 | tf_op jit(solution)/shard_map/ppermute | solution.py:51
  26.3 0.0 copy-done.2
  26.3 0.0 copy-start.1
  26.3 2.0 %fusion.2 = bf16[16,5,10,256]{3,0,2,1:T(8,128)(2,1)S(1)} fusion(bf16[16,7,12,256]{3,0,2,1:T(8,128)(2,1)S(1)} %reshape.160, f32[1,5,10,256]{3,0,2,1:T(1,128)S(1)} %slice.498, f32[2,5,10,256]{3,0,2,1:T(2,128)S(1)} %slice.497, f32[3,5,10,256]{3,0,2,1:T(4,128)S(1)} %slice.496, f32[4,5,10,256]{3,0,2,1:T(4,128)S(1)} %slice.495, f32[5,5,10,256]{3,0,2,1:T(8,128)S(1)} %slice.494, ...), kind=kOutput, calls=%fused_computation.3 | convolution fusion | flops 112435200 | bytes 9721856 | tf_op jit(solution)/shard_map/dot_general | solution.py:30
  28.3 0.0 collective-permute-done
  28.4 3.4 %collective-permute-done.1 = bf16[16,7,2,256]{3,0,2,1:T(8,128)(2,1)S(1)} collective-permute-done((bf16[16,7,2,256]{3,0,2,1:T(8,128)(2,1)S(1)}, bf16[16,7,2,256]{3,0,2,1:T(8,128)(2,1)S(1)}, u32[]{:S(2)}, u32[]{:S(2)}) %collective-permute-start.1) | collective-permute-done | bytes 114720 | tf_op jit(solution)/shard_map/ppermute | solution.py:51
  31.7 0.0 copy-done.1
  31.7 1.1 %fusion.23 = f32[16,5,10,256]{3,0,2,1:T(8,128)S(1)} fusion(bf16[2,3,3,256,256]{4,3,2,1,0:T(8,128)(2,1)S(1)} %copy-done.1, bf16[16,7,2,256]{3,0,2,1:T(8,128)(2,1)S(1)} %collective-permute-done.1, bf16[16,7,4,256]{3,0,2,1:T(8,128)(2,1)S(1)} %get-tuple-element.8, bf16[16,7,4,256]{3,0,2,1:T(8,128)(2,1)S(1)} %get-tuple-element.7, ...), kind=kOutput, calls=%fused_computation.25 | convolution fusion | flops 945979392 | bytes 2686976 | tf_op jit(solution)/shard_map/conv_general_dilated | solution.py:10
  33.1 2.3 %add_convert_fusion.1 = bf16[16,5,10,256]{3,0,2,1:T(8,128)(2,1)S(1)} fusion(bf16[16,7,2,256]{3,0,2,1:T(8,128)(2,1)S(1)} %collective-permute-done.1, bf16[16,7,4,256]{3,0,2,1:T(8,128)(2,1)S(1)} %get-tuple-element.8, bf16[16,7,4,256]{3,0,2,1:T(8,128)(2,1)S(1)} %get-tuple-element.7, bf16[16,7,2,256]{3,0,2,1:T(8,128)(2,1)S(1)} %collective-permute-done, ...), kind=kOutput, calls=%fused_computation.22 | convolution fusion | flops 113049600 | bytes 10000384 | tf_op jit(solution)/shard_map/dot_general | solution.py:30
  35.5 0.1 maximum_select_fusion
  35.6 0.9 %fusion.35 = f32[16,3,12,256]{3,0,2,1:T(8,128)S(1)} fusion(bf16[16,5,14,256]{3,0,2,1:T(8,128)(2,1)S(1)} %maximum_select_fusion, bf16[2,3,3,256,256]{4,3,2,1,0:T(8,128)(2,1)S(1)} %copy-done.1), kind=kOutput, calls=%fused_computation.36 | convolution fusion | flops 680361984 | bytes 2342912 | tf_op jit(solution)/shard_map/conv_general_dilated | solution.py:10
  36.8 1.4 %fusion.6 = bf16[16,3,12,256]{3,0,2,1:T(8,128)(2,1)S(1)} fusion(bf16[16,5,14,256]{3,0,2,1:T(8,128)(2,1)S(1)} %maximum_select_fusion, f32[1,3,12,256]{3,0,2,1:T(1,128)S(1)} %slice.515, f32[2,3,12,256]{3,0,2,1:T(2,128)S(1)} %slice.514, f32[3,3,12,256]{3,0,2,1:T(4,128)S(1)} %slice.513, f32[4,3,12,256]{3,0,2,1:T(4,128)S(1)} %slice.512, ...), kind=kOutput, calls=%fused_computation.9 | convolution fusion | flops 80953344 | bytes 7041024 | tf_op jit(solution)/shard_map/dot_general | solution.py:30
  38.2 0.1 slice_bitcast_fusion.5
  38.3 0.3 pad_maximum_fusion.1
  38.6 8.7 %all_to_all.10 = bf16[4,4,3,12,256]{4,1,3,2,0:T(4,128)(2,1)S(1)} all-to-all(bf16[4,4,3,12,256]{4,1,3,2,0:T(4,128)(2,1)S(1)} %pad_maximum_fusion.1), channel_id=1, replica_groups=mesh['groups'=2,'tm'=4,'width'=4] {'tm'}, dimensions={0} | all-to-all | bytes 589824 | tf_op jit(solution)/shard_map/all_to_all | solution.py:68
  47.3 0.7 %copy.9 = bf16[4,12,12,256]{3,0,2,1:T(4,128)(2,1)} copy(bf16[4,12,12,256]{3,0,2,1:T(4,128)(2,1)S(1)} %bitcast.133) | data formatting | bytes 589824
  (31 shorter events, 0.7 us)
Async XLA Ops:
  0.0 7.2 %copy-start = (f32[2,16,256]{2,1,0:T(8,128)S(1)}, f32[2,16,256]{2,1,0:T(8,128)}, u32[]{:S(2)}) copy-start(f32[2,16,256]{2,1,0:T(8,128)} %param.6) | copy-start | bytes 98308
  2.9 14.8 %all-to-all-start = ((bf16[4,4,7,12,256]{4,1,3,2,0:T(4,128)(2,1)}), bf16[4,4,7,12,256]{4,1,3,2,0:T(4,128)(2,1)S(1)}, u32[]{:S(2)}, u32[]{:S(2)}) async-start(bf16[4,4,7,12,256]{4,1,3,2,0:T(4,128)(2,1)} %pad_maximum_fusion), calls=%async_computation | async-start | bytes 1376256 | tf_op jit(solution)/shard_map/all_to_all | solution.py:46
  20.5 5.8 %copy-start.2 = (bf16[2,256,256]{2,1,0:T(8,128)(2,1)S(1)}, bf16[2,256,256]{2,1,0:T(8,128)(2,1)}, u32[]{:S(2)}) copy-start(bf16[2,256,256]{2,1,0:T(8,128)(2,1)} %param.7) | copy-start | bytes 786436
  20.8 7.5 %collective-permute-start = (bf16[16,7,2,256]{3,0,2,1:T(8,128)(2,1)S(1)}, bf16[16,7,2,256]{3,0,2,1:T(8,128)(2,1)S(1)}, u32[]{:S(2)}, u32[]{:S(2)}) collective-permute-start(bf16[16,7,2,256]{3,0,2,1:T(8,128)(2,1)S(1)} %get-tuple-element.5), channel_id=1, source_target_pairs={{0,1},{1,2},{2,3},{4,5},{5,6},{6,7},{8,9},{9,10},{10,11},{12,13},{... | collective-permute-start | bytes 344072 | tf_op jit(solution)/shard_map/ppermute | solution.py:50
  25.0 6.7 %collective-permute-start.1 = (bf16[16,7,2,256]{3,0,2,1:T(8,128)(2,1)S(1)}, bf16[16,7,2,256]{3,0,2,1:T(8,128)(2,1)S(1)}, u32[]{:S(2)}, u32[]{:S(2)}) collective-permute-start(bf16[16,7,2,256]{3,0,2,1:T(8,128)(2,1)S(1)} %get-tuple-element.6), channel_id=1, source_target_pairs={{1,0},{2,1},{3,2},{5,4},{6,5},{7,6},{9,8},{10,9},{11,10},{13,12},{... | collective-permute-start | bytes 344072 | tf_op jit(solution)/shard_map/ppermute | solution.py:51
  26.3 5.4 %copy-start.1 = (bf16[2,3,3,256,256]{4,3,2,1,0:T(8,128)(2,1)S(1)}, bf16[2,3,3,256,256]{4,3,2,1,0:T(8,128)(2,1)}, u32[]{:S(2)}) copy-start(bf16[2,3,3,256,256]{4,3,2,1,0:T(8,128)(2,1)} %param.5) | copy-start | bytes 7077892
